TPU v7x, 32 devices: a whole 2x2x4 slice. The times are simulated.
32 devices in a mesh: row: 4 (over z), col: 8 (over y, x, core).
Axes of the slice: x: 2, y: 2, z: 4, core: 2. Of those that a mesh axis runs over, the one named last changes fastest.
Arguments:
- factor_rows: float32 [2, 1024, 4096], P(None, 'col', 'row'), as said below
- adjoint_rows: float32 [2, 1024, 4096], P(None, 'col', 'row'), as said below
- panel_inverse: float32 [2, 1024, 1024], replicated, as said below
Outputs:
- kernel_adjoint: float32 [2, 1024, 4096], P(None, 'col', 'row')
Inputs may be any that keep to these rules, and one draw needn't show every extreme that they name: `factor_rows`: zero right of the diagonal; in panel p the columns J_p hold a lower-triangular block with diagonal entries from 0.5 to 4. `adjoint_rows`: zero right of the diagonal of the same rows. panel_inverse[p] is the inverse of factor_rows[p, :, J_p] to float32 rounding.
All inputs are finite; a program needn't handle non-finite values.
Results may differ from a plain program's by a relative error of at most 0.0001.
Values sent between devices are 32-bit elements; how exact they have to be, the bound alone decides.
No kernel may reach another device: no remote copies, remote signals or barrier semaphores. Data moves between devices by JAX's collectives and lax.ppermute only.
A program may use at most 128 MiB of HBM per device.

v0:
```python
import jax
import jax.numpy as jnp
from jax import lax
from jax.sharding import PartitionSpec as P

HIGHEST = lax.Precision.HIGHEST


def spread(value, axis, source):
    kept = jnp.where(lax.axis_index(axis) == source, value, 0).astype(value.dtype)
    return lax.psum(kept, axis)


def phi_lower(matrix):
    unit_diag = jnp.eye(matrix.shape[0], dtype=jnp.float32)
    return jnp.tril(matrix) * (1.0 - 0.5 * unit_diag)


def product(left_mat, right_mat):
    return jnp.dot(left_mat, right_mat, precision=HIGHEST, preferred_element_type=jnp.float32)


def diag_fix(factor, diag_pre, inverse):
    inner = phi_lower(product(factor.T, diag_pre))
    return phi_lower(product(product(inverse.T, inner + inner.T), inverse))


def fixed_block(factor, diag_term, inverse):
    diag_pre = jnp.tril(lax.psum(diag_term, "col"))
    return diag_fix(factor, diag_pre, inverse)


def local(factor_rows, adjoint_rows, panel_inverse):
    row_count = lax.axis_size("row")
    panels = panel_inverse.shape[0]
    panel_width = panel_inverse.shape[1]
    slab_rows = factor_rows.shape[1]
    span_cols = factor_rows.shape[2]
    row_pos = lax.axis_index("row")
    col_pos = lax.axis_index("col")
    first_col = (row_count - panels) * panel_width
    columns = row_pos * span_cols + jnp.arange(span_cols, dtype=jnp.int32)
    offset = col_pos * slab_rows
    adjoint = adjoint_rows
    for panel in range(panels - 1, -1, -1):
        owner_row = row_count - panels + panel
        is_owner = row_pos == owner_row
        inverse = panel_inverse[panel]
        held_adj, held_fac = (
            spread(adjoint[panel:], "row", owner_row),
            spread(factor_rows[panel:], "row", owner_row),
        )
        col_adjoint = jnp.einsum("qib,bj->qij", held_adj[1:], inverse, precision=HIGHEST)
        placed = lax.dynamic_update_slice(
            jnp.zeros((panel_width, panel_width), jnp.float32), held_adj[0], (offset, 0)
        )
        diag_term = placed - jnp.einsum("qbi,qbj->ij", col_adjoint, held_fac[1:], precision=HIGHEST)
        row_panel = lax.all_gather(factor_rows[panel], "col", axis=0, tiled=True)
        diag_factor = lax.all_gather(held_fac[0], "col", axis=0, tiled=True)
        diag_new = fixed_block(diag_factor, diag_term, inverse)
        sym_rows = lax.dynamic_slice_in_dim(diag_new + diag_new.T, offset, slab_rows, 0)
        left_cols = (columns < first_col + panel * panel_width)[None, :]
        row_update = product(sym_rows, row_panel)
        pieces = [adjoint[:panel]]
        if panel + 1 < panels:
            later_rows = factor_rows[panel + 1 :]
            row_update = (
                lax.psum_scatter(
                    jnp.einsum("qbi,qbj->ij", col_adjoint, later_rows, precision=HIGHEST),
                    "col",
                    scatter_dimension=0,
                    tiled=True,
                )
                + row_update
            )
            block_update = jnp.einsum("qib,bj->qij", col_adjoint, row_panel, precision=HIGHEST)
            lower_new = jnp.where(
                left_cols[None], adjoint[panel + 1 :] - block_update, adjoint[panel + 1 :]
            )
            lower_new = jnp.where(is_owner, col_adjoint, lower_new)
        own_new = jnp.where(left_cols, adjoint[panel] - row_update, adjoint[panel])
        own_new = jnp.where(
            is_owner, lax.dynamic_slice_in_dim(diag_new, offset, slab_rows, 0), own_new
        )
        pieces.append(own_new[None])
        if panel + 1 < panels:
            pieces.append(lower_new)
        adjoint = jnp.concatenate(pieces, axis=0)
    return adjoint


def solution(mesh):
    return jax.shard_map(
        local,
        mesh=mesh,
        in_specs=(P(None, "col", "row"), P(None, "col", "row"), P()),
        out_specs=P(None, "col", "row"),
        check_vma=False,
    )
```

profile of v0, /device:TPU:0, one launch (start us, length us, event | category | flops | bytes accessed | tf_op | source)
XLA Modules:
  0.0 607.5 jit_solution(6495797042716820309)
XLA Ops:
  11.5 55.0 %all-reduce.13.cloned.1.call-done = (f32[128,1024]{0,1:T(8,128)}, f32[128,1024]{0,1:T(8,128)}) async-done(((f32[128,1024]{0,1:T(8,128)}, f32[128,1024]{0,1:T(8,128)}), (f32[128,1024]{0,1:T(8,128)}, f32[128,1024]{0,1:T(8,128)})) %all-reduce.13.cloned.1.call-update) | async-done | bytes 1048592 | tf_op jit(solution)/shard_map/psum | solution.py:11
  73.8 76.7 %all-reduce.7.cloned.1.call-done = f32[1024,1024]{0,1:T(8,128)} async-done(((f32[1024,1024]{0,1:T(8,128)}), f32[1024,1024]{0,1:T(8,128)}) %all-reduce.7.cloned.1.call-update) | async-done | bytes 4194320 | tf_op jit(solution)/shard_map/psum | solution.py:29
  150.6 39.4 %all-gather.8.cloned.1.call-done = f32[1024,1024]{0,1:T(8,128)} async-done(((f32[128,1024]{0,1:T(8,128)}), f32[1024,1024]{0,1:T(8,128)}) %all-gather.8.cloned.1.call-update) | async-done | bytes 4194320 | tf_op jit(solution)/shard_map/all_gather | solution.py:59
  190.0 17.9 %fusion.29 = f32[1024,1024]{1,0:T(8,128)} fusion(f32[1024,1024]{0,1:T(8,128)} %all-gather.8.cloned.1.call-done, f32[1024,1024]{0,1:T(8,128)} %all-reduce.7.cloned.1.call-done), kind=kOutput, calls=%fused_computation.36 | convolution fusion | flops 12886999040 | bytes 12582912 | tf_op jit(solution)/shard_map/dot_general | solution.py:20
  207.8 5.3 copy.8
  213.2 20.0 %fusion.17 = f32[1024,1024]{1,0:T(8,128)S(1)} fusion(f32[1024,1024]{1,0:T(8,128)} %fusion.29, f32[1024,1024]{0,1:T(8,128)} %copy.8, f32[2,1024,1024]{2,1,0:T(8,128)} %param.5), kind=kOutput, calls=%fused_computation.17 | convolution fusion | flops 12898533376 | bytes 16777216 | tf_op jit(solution)/shard_map/dot_general | solution.py:20
  233.2 17.1 %fusion.15 = f32[1024,1024]{1,0:T(8,128)} fusion(f32[1024,1024]{1,0:T(8,128)S(1)} %fusion.17, f32[2,1024,1024]{2,1,0:T(8,128)} %param.5), kind=kOutput, calls=%fused_computation.15 | convolution fusion | flops 12884901888 | bytes 12582912 | tf_op jit(solution)/shard_map/dot_general | solution.py:20
  250.3 5.3 copy.9
  255.7 6.5 %select_multiply_fusion.1 = (f32[1024,1024]{0,1:T(8,128)}, f32[1024,1024]{0,1:T(8,128)}) fusion(f32[1024,1024]{0,1:T(8,128)} %copy.9), kind=kLoop, calls=%fused_computation.28 | loop fusion | flops 9437184 | bytes 12582912 | tf_op jit(solution)/shard_map/mul | solution.py:16
  262.2 6.2 %fusion.50 = f32[128,1024]{0,1:T(8,128)S(1)} fusion(f32[1,1024,1024]{1,2,0:T(8,128)} %all-gather.12.cloned.1.call-done, f32[1024,1024]{0,1:T(8,128)} %bitcast.96, s32[]{:T(128)S(6)} %select_n.105, f32[1024,1024]{0,1:T(8,128)} %get-tuple-element.13, f32[1,128,1024]{1,2,0:T(8,128)S(1)} %copy.23, f32[1024,1024]{0,1:T(8,128)} %get-tuple-element.14, ...), kind=kOutput, calls=%fused_computation.55 | convolution fusion | flops 1611399168 | bytes 7473664 | tf_op jit(solution)/shard_map/dot_general | solution.py:20
  271.7 85.6 %all-reduce.11.cloned.1.call-done = (f32[2,128,1024]{1,2,0:T(8,128)}, f32[2,128,1024]{1,2,0:T(8,128)}) async-done(((f32[2,128,1024]{1,2,0:T(8,128)}, f32[2,128,1024]{1,2,0:T(8,128)}), (f32[2,128,1024]{1,2,0:T(8,128)}, f32[2,128,1024]{1,2,0:T(8,128)})) %all-reduce.11.cloned.1.call-update) | async-done | bytes 2097168 | tf_op jit(solution)/shard_map/psum | solution.py:11
  358.5 4.8 fusion.11
  363.3 5.1 convolution_subtract_fusion
  370.4 5.0 fusion.89
  375.7 19.2 %all-gather.14.cloned.1.call-done = f32[1,1024,1024]{2,1,0:T(8,128)} async-done(((f32[1,128,1024]{2,1,0:T(8,128)}), f32[1,1024,1024]{2,1,0:T(8,128)}) %all-gather.14.cloned.1.call-update) | async-done | bytes 4194320 | tf_op jit(solution)/shard_map/all_gather | solution.py:58
  394.8 8.7 %fusion.65 = f32[1,128,1024]{1,2,0:T(8,128)S(1)} fusion(f32[128,1024]{0,1:T(8,128)S(1)} %copy.16, f32[128,1024]{0,1:T(8,128)S(1)} %fusion.50, f32[128,1024]{1,0:T(8,128)S(1)} %fusion.11, f32[1,1024,1024]{2,1,0:T(8,128)} %all-gather.14.cloned.1.call-done, pred[1024]{0:T(1024)(128)(4,1)S(1)} %fusion.97, pred[]{:T(512)S(6)} %eq.34), kind=kOutput, calls=%fused_computation.60 | convolution fusion | flops 1611005952 | bytes 6292481 | tf_op jit(solution)/shard_map/qib,bj->qij/dot_general | solution.py:76
  403.5 76.0 %all-reduce.9.cloned.1.call-done = f32[1024,1024]{0,1:T(8,128)} async-done(((f32[1024,1024]{0,1:T(8,128)}), f32[1024,1024]{0,1:T(8,128)}) %all-reduce.9.cloned.1.call-update) | async-done | bytes 4194320 | tf_op jit(solution)/shard_map/psum | solution.py:29
  479.5 39.4 %all-gather.10.cloned.1.call-done = f32[1,1024,1024]{1,2,0:T(8,128)} async-done(((f32[1,128,1024]{1,2,0:T(8,128)}), f32[1,1024,1024]{1,2,0:T(8,128)}) %all-gather.10.cloned.1.call-update) | async-done | bytes 4194320 | tf_op jit(solution)/shard_map/all_gather | solution.py:59
  518.9 17.9 %fusion.22 = f32[1024,1024]{1,0:T(8,128)} fusion(f32[1,1024,1024]{1,2,0:T(8,128)} %all-gather.10.cloned.1.call-done, f32[1024,1024]{0,1:T(8,128)} %all-reduce.9.cloned.1.call-done), kind=kOutput, calls=%fused_computation.22 | convolution fusion | flops 12886999040 | bytes 12582912 | tf_op jit(solution)/shard_map/dot_general | solution.py:20
  536.8 5.3 copy.11
  542.1 20.4 %fusion.6 = f32[1024,1024]{1,0:T(8,128)S(1)} fusion(f32[1024,1024]{1,0:T(8,128)} %fusion.22, f32[1024,1024]{0,1:T(8,128)} %copy.11, f32[2,1024,1024]{2,1,0:T(8,128)} %param.5), kind=kOutput, calls=%fused_computation.7 | convolution fusion | flops 12898533376 | bytes 16777216 | tf_op jit(solution)/shard_map/dot_general | solution.py:20
  562.5 17.0 %fusion.8 = f32[1024,1024]{1,0:T(8,128)} fusion(f32[1024,1024]{1,0:T(8,128)S(1)} %fusion.6, f32[2,1024,1024]{2,1,0:T(8,128)} %param.5), kind=kOutput, calls=%fused_computation.8 | convolution fusion | flops 12884901888 | bytes 12582912 | tf_op jit(solution)/shard_map/dot_general | solution.py:20
  579.5 5.5 copy.12
  589.7 9.7 %fusion.77 = f32[1,128,1024]{1,2,0:T(8,128)S(1)} fusion(f32[128,1024]{0,1:T(8,128)} %reduce-scatter.2.cloned.1.call-done, f32[1,1024,1024]{2,1,0:T(8,128)} %all-gather.14.cloned.1.call-done, f32[1024,1024]{0,1:T(8,128)} %bitcast.95, s32[]{:T(128)S(6)} %select_n.105, f32[1024,1024]{0,1:T(8,128)} %select_multiply_fusion, f32[1,128,1024]{1,2,0:T(8,128)S(1)} %copy.22, ...), kind=kOutput, calls=%fused_computation.64 | convolution fusion | flops 1611530240 | bytes 7997952 | tf_op jit(solution)/shard_map/dot_general | solution.py:20
  (47 shorter events, 25.0 us)
Async XLA Ops:
  6.5 60.0 %all-reduce.13.cloned.1.call-start = ((), (), s32[]{:S(2)}) async-start(), calls=%async_computation.9 | async-start | bytes 2097152 | tf_op jit(solution)/shard_map/psum | solution.py:11
  11.5 139.1 %all-reduce.7.cloned.1.call-start = ((), (), s32[]{:S(2)}) async-start(), calls=%async_computation.2 | async-start | bytes 8388608 | tf_op jit(solution)/shard_map/psum | solution.py:29
  66.5 2.5 copy-start.2
  69.9 120.1 %all-gather.8.cloned.1.call-start = ((), (), s32[]{:S(2)}) async-start(), calls=%async_computation.1 | async-start | bytes 4718592 | tf_op jit(solution)/shard_map/all_gather | solution.py:59
  70.6 191.5 %all-gather.12.cloned.1.call-start = ((), (), s32[]{:S(2)}) async-start(), calls=%async_computation.6 | async-start | bytes 4718592 | tf_op jit(solution)/shard_map/all_gather | solution.py:58
  71.2 286.0 %all-reduce.11.cloned.1.call-start = ((), (), s32[]{:S(2)}) async-start(), calls=%async_computation.8 | async-start | bytes 4194304 | tf_op jit(solution)/shard_map/psum | solution.py:11
  269.5 125.4 %all-gather.14.cloned.1.call-start = ((), (), s32[]{:S(2)}) async-start(), calls=%async_computation.7 | async-start | bytes 4718592 | tf_op jit(solution)/shard_map/all_gather | solution.py:58
  271.4 208.0 %all-reduce.9.cloned.1.call-start = ((), (), s32[]{:S(2)}) async-start(), calls=%async_computation.3 | async-start | bytes 8388608 | tf_op jit(solution)/shard_map/psum | solution.py:29
  357.2 1.2 copy-start.1
  358.4 4.8 copy-start
  368.4 150.5 %all-gather.10.cloned.1.call-start = ((), (), s32[]{:S(2)}) async-start(), calls=%async_computation.5 | async-start | bytes 4718592 | tf_op jit(solution)/shard_map/all_gather | solution.py:59
  370.4 219.3 %reduce-scatter.2.cloned.1.call-start = ((), (), s32[]{:S(2)}) async-start(), calls=%async_computation.4 | async-start | bytes 4718592 | tf_op jit(solution)/shard_map/reduce_scatter | solution.py:68
Sparse Core Ops, SparseCore 0:
  11.6 54.8 all-reduce.12
  70.1 80.3 all-reduce.6
  152.4 37.4 all-gather.7
  191.7 37.4 all-gather.11
  269.6 87.5 all-reduce.10
  359.1 35.6 all-gather.13
  398.5 80.9 all-reduce.8
  481.4 37.4 all-gather.9
  522.3 51.3 reduce-scatter.1
where the time goes:
time: 614 us; the launch traced here: 608 us
  waiting for transfers between devices  393 us (64%)
  matrix products  150 us (24%)
  local copies, waits for them, and re-layouts  34.6 us (6%)
  other arithmetic  16.5 us (3%)
  between operations  13.6 us (2%)
    psum x2, waiting for transfers between devices, fixed_block(): diag_pre = jnp.tril(lax.psum(diag_term, 'col'))  153 us
    psum x2, waiting for transfers between devices, spread(): return lax.psum(kept, axis)  141 us
    dot_general x8, matrix products, product(): jnp.dot(left_mat, right_mat, precision=HIGHEST, preferred_element_type=jn...  126 us
    all_gather x2, waiting for transfers between devices, local(): diag_factor = lax.all_gather(held_fac[0], 'col', axis=0, tiled=True)  78.8 us
    dot_general x4, local copies, waits for them, and re-layouts, product(): jnp.dot(left_mat, right_mat, precision=HIGHEST, preferred_element_type=jn...  21.5 us
    all_gather x2, waiting for transfers between devices, local(): row_panel = lax.all_gather(factor_rows[panel], 'col', axis=0, tiled=True)  19.2 us
  transfers between devices with their start and end apart: 9, of which 7 were waited for; matrix products, arithmetic and copies ran while one was open for 29% of the time, Pallas kernels for 0%

commit v1 on v0

v1 whole, which is shorter than its diff:
```python
import jax
import jax.numpy as jnp
from jax import lax
from jax.sharding import PartitionSpec as P

HIGHEST = lax.Precision.HIGHEST


def mm(left, right):
    return jnp.dot(left, right, precision=HIGHEST, preferred_element_type=jnp.float32)


def tmm(left, right):
    return lax.dot_general(left, right, (((0,), (0,)), ((), ())), precision=HIGHEST,
                           preferred_element_type=jnp.float32)


def phi_sym(matrix):
    eye = jnp.eye(matrix.shape[0], dtype=jnp.float32)
    half = jnp.tril(matrix) * (1.0 - 0.5 * eye)
    return half + half.T


def row_bcast(value, source, targets):
    row = lax.axis_index("row")
    recv = None
    for target in targets:
        got = lax.ppermute(value, "row", [(source, target)])
        recv = got if recv is None else recv + got
    if recv is None:
        return value
    return jnp.where(row == source, value, recv)


def local(factor_rows, adjoint_rows, panel_inverse):
    row_count = lax.axis_size("row")
    panels = panel_inverse.shape[0]
    width = panel_inverse.shape[1]
    slab = factor_rows.shape[1]
    assert panels == 2 and factor_rows.shape[2] == width
    row = lax.axis_index("row")
    offset = lax.axis_index("col") * slab
    own1 = row_count - 1
    own0 = row_count - 2

    grow = offset + jnp.arange(slab, dtype=jnp.int32)[:, None]
    gcol = jnp.arange(width, dtype=jnp.int32)[None, :]
    lower = gcol <= grow
    diag_scale = jnp.where(gcol == grow, 0.5, 1.0).astype(jnp.float32)

    f0, f1 = factor_rows[0], factor_rows[1]
    a0, a1 = adjoint_rows[0], adjoint_rows[1]
    inv0, inv1 = panel_inverse[0], panel_inverse[1]

    x1 = tmm(f1, jnp.where(lower, a1, 0.0))
    q1 = lax.psum_scatter(phi_sym(x1), "col", scatter_dimension=0, tiled=True)
    w1 = mm(q1, inv1)
    v1 = lax.psum_scatter(tmm(lax.dynamic_slice_in_dim(inv1, offset, slab, 0), w1), "col",
                          scatter_dimension=0, tiled=True)
    diag1 = jnp.where(lower, v1, 0.0) * diag_scale
    gathered_in, v1 = lax.optimization_barrier((factor_rows, v1))
    full = lax.all_gather(gathered_in, "col", axis=1, tiled=True)
    v1 = row_bcast(v1, own1, list(range(own1)))
    full, v1 = lax.optimization_barrier((full, v1))
    a1_left = a1 - mm(v1, full[1])

    col_adj = mm(a1_left, inv0)
    col_adj = row_bcast(col_adj, own0, list(range(own0)))
    cross = tmm(col_adj, f1)
    x0 = tmm(f0, jnp.where(lower, a0, 0.0)) - tmm(full[0], jnp.tril(cross))
    summed = lax.psum_scatter(jnp.where(row == own0, phi_sym(x0), cross), "col",
                              scatter_dimension=0, tiled=True)
    w0 = mm(summed, inv0)
    v0 = lax.psum_scatter(tmm(lax.dynamic_slice_in_dim(inv0, offset, slab, 0), w0), "col",
                          scatter_dimension=0, tiled=True)
    diag0 = jnp.where(lower, v0, 0.0) * diag_scale
    v0 = row_bcast(v0, own0, list(range(own0)))

    left1 = a1_left - mm(col_adj, full[0])
    left0 = a0 - summed - mm(v0, full[0])
    out1 = jnp.where(row < own0, left1, jnp.where(row == own0, col_adj, diag1))
    out0 = jnp.where(row < own0, left0, jnp.where(row == own0, diag0, a0))
    return jnp.stack([out0, out1])


def solution(mesh):
    return jax.shard_map(
        local,
        mesh=mesh,
        in_specs=(P(None, "col", "row"), P(None, "col", "row"), P()),
        out_specs=P(None, "col", "row"),
        check_vma=False,
    )
```

time: 614 us -> 434 us (0.71)
  waiting for transfers between devices: 393 us -> 285 us
  matrix products: 150 us -> 74.6 us
  starting transfers between devices: 0.5 us -> 8.54 us
  local copies, waits for them, and re-layouts: 34.6 us -> 26.6 us
    psum x4 -> x0, waiting for transfers between devices: 293 us -> none  [the longest x2 153 us: fixed_block(): diag_pre = jnp.tril(lax.psum(diag_term, 'col'))]
    reduce_scatter x1 -> x4, waiting for transfers between devices: 0.01 us -> 197 us  [the longest x1 51.5 us: local(): lax.psum_scatter(tmm(lax.dynamic_slice_in_dim(inv0, offset, slab, 0), w0)...]
    all_gather x4 -> x1, waiting for transfers between devices: 98 us -> 16 us  [local(): full = lax.all_gather(gathered_in, 'col', axis=1, tiled=True)]
    dot_general x12, matrix products: 150 us -> 74.6 us  [the longest x6 45.7 us: tmm(): lax.dot_general(left, right, (((0,), (0,)), ((), ())), precision=HIGHEST,...]
    ppermute x0 -> x7, waiting for transfers between devices: none -> 72 us  [row_bcast(): got = lax.ppermute(value, 'row', [(source, target)])]
    mul x2 -> x0, other arithmetic: 11.2 us -> none  [phi_lower(): return jnp.tril(matrix) * (1.0 - 0.5 * unit_diag)]
    select_n x2, other arithmetic: 2.13 us -> 10.8 us  [the longest x1 10.7 us: local(): jnp.where(row == own0, phi_sym(x0), cross)]
    ppermute x0 -> x7, starting transfers between devices: none -> 8.37 us  [row_bcast(): got = lax.ppermute(value, 'row', [(source, target)])]
  transfers between devices with their start and end apart: 9 -> 12, of which waited for: 7 -> 8; matrix products, arithmetic and copies ran while one was open for 29% -> 6% of each run, Pallas kernels for 0% -> 0%
where the time goes in v1:
time: 434 us; the launch traced here: 427 us
  waiting for transfers between devices  285 us (66%)
  matrix products  74.6 us (17%)
  local copies, waits for them, and re-layouts  26.6 us (6%)
  other arithmetic  18.1 us (4%)
  between operations  13.8 us (3%)
  starting transfers between devices  8.54 us (2%)
    ppermute x7, waiting for transfers between devices, row_bcast(): got = lax.ppermute(value, 'row', [(source, target)])  72 us
    reduce_scatter x1, waiting for transfers between devices, local(): lax.psum_scatter(tmm(lax.dynamic_slice_in_dim(inv0, offset, slab, 0), w0)...  51.5 us
    reduce_scatter x1, waiting for transfers between devices, local(): lax.psum_scatter(tmm(lax.dynamic_slice_in_dim(inv1, offset, slab, 0), w1)...  51.4 us
    reduce_scatter x1, waiting for transfers between devices, local(): lax.psum_scatter(jnp.where(row == own0, phi_sym(x0), cross), 'col', scatt...  48.7 us
    dot_general x6, matrix products, tmm(): lax.dot_general(left, right, (((0,), (0,)), ((), ())), precision=HIGHEST,...  45.7 us
    reduce_scatter x1, waiting for transfers between devices, local(): q1 = lax.psum_scatter(phi_sym(x1), 'col', scatter_dimension=0, tiled=True)  45.6 us
    dot_general x6, matrix products, mm(): jnp.dot(left, right, precision=HIGHEST, preferred_element_type=jnp.float32)  28.9 us
    dot_general x3, local copies, waits for them, and re-layouts, tmm(): lax.dot_general(left, right, (((0,), (0,)), ((), ())), precision=HIGHEST,...  16.2 us
  transfers between devices with their start and end apart: 12, of which 8 were waited for; matrix products, arithmetic and copies ran while one was open for 6% of the time, Pallas kernels for 0%

profile of v1, /device:TPU:0, one launch (start us, length us, event | category | flops | bytes accessed | tf_op | source)
XLA Modules:
  0.0 426.9 jit_solution(11537045174155950510)
XLA Ops:
  6.5 6.7 %fusion.55 = f32[1024,1024]{1,0:T(8,128)} fusion(f32[2,128,1024]{2,1,0:T(8,128)} %param.3, f32[2,128,1024]{2,1,0:T(8,128)} %param.4, s32[128]{0:T(128)S(1)} %iota_add_fusion), kind=kOutput, calls=%fused_computation.53 | convolution fusion | flops 1610874880 | bytes 5243392 | tf_op jit(solution)/shard_map/dot_general | solution.py:14
  13.2 5.4 %copy.5 = f32[1024,1024]{0,1:T(8,128)} copy(f32[1024,1024]{1,0:T(8,128)} %fusion.55) | data formatting | bytes 8388608 | tf_op jit(solution)/shard_map/dot_general | solution.py:14
  18.6 6.2 %fusion.19 = f32[1024,1024]{1,0:T(8,128)} fusion(f32[1024,1024]{0,1:T(8,128)} %copy.5, f32[1024,1024]{1,0:T(8,128)} %fusion.55), kind=kLoop, calls=%fused_computation.21 | loop fusion | flops 13631488 | bytes 12582912 | tf_op jit(solution)/shard_map/add | solution.py:21
  24.9 8.5 %fusion.87 = (f32[1,1024,1024]{2,1,0:T(8,128)}, f32[1,1024,1024]{2,1,0:T(8,128)}) fusion(f32[2,1024,1024]{2,1,0:T(8,128)} %param.5), kind=kLoop, calls=%fused_computation.92 | loop fusion | bytes 16777216 | tf_op jit(solution)/shard_map/slice | solution.py:53
  33.4 45.6 %reduce-scatter.5.cloned.1.call-done = f32[128,1024]{1,0:T(8,128)} async-done(((f32[1024,1024]{1,0:T(8,128)}), f32[128,1024]{1,0:T(8,128)}) %reduce-scatter.5.cloned.1.call-update) | async-done | bytes 524304 | tf_op jit(solution)/shard_map/reduce_scatter | solution.py:56
  79.0 4.8 %fusion.16 = f32[128,1024]{1,0:T(8,128)S(1)} fusion(f32[128,1024]{1,0:T(8,128)} %reduce-scatter.5.cloned.1.call-done, f32[2,1024,1024]{2,1,0:T(8,128)} %param.5), kind=kOutput, calls=%fused_computation.17 | convolution fusion | flops 1610612736 | bytes 5242880 | tf_op jit(solution)/shard_map/dot_general | solution.py:10
  83.8 6.1 %fusion.58 = f32[1024,1024]{1,0:T(8,128)} fusion(f32[128,1024]{1,0:T(8,128)S(1)} %fusion.16, f32[1,1024,1024]{2,1,0:T(8,128)} %get-tuple-element.14, s32[]{:T(128)S(6)} %select_n.91), kind=kOutput, calls=%fused_computation.56 | convolution fusion | flops 1610612736 | bytes 5242884 | tf_op jit(solution)/shard_map/dot_general | solution.py:14
  90.0 51.4 %reduce-scatter.7.cloned.1.call-done = f32[128,1024]{1,0:T(8,128)} async-done(((f32[1024,1024]{1,0:T(8,128)}), f32[128,1024]{1,0:T(8,128)}) %reduce-scatter.7.cloned.1.call-update) | async-done | bytes 524304 | tf_op jit(solution)/shard_map/reduce_scatter | solution.py:58
  144.4 37.2 %collective-permute-done = f32[128,1024]{1,0:T(8,128)S(1)} collective-permute-done((f32[128,1024]{1,0:T(8,128)}, f32[128,1024]{1,0:T(8,128)S(1)}, u32[]{:S(2)}, u32[]{:S(2)}) %collective-permute-start) | collective-permute-done | bytes 524320 | tf_op jit(solution)/shard_map/ppermute | solution.py:28
  181.7 16.0 %all-gather.2.cloned.1.call-done = f32[2,1024,1024]{2,1,0:T(8,128)} async-done(((f32[2,128,1024]{2,1,0:T(8,128)}), f32[2,1024,1024]{2,1,0:T(8,128)}) %all-gather.2.cloned.1.call-update) | async-done | bytes 8388624 | tf_op jit(solution)/shard_map/all_gather | solution.py:62
  209.7 5.2 %fusion.60 = f32[1024,1024]{1,0:T(8,128)} fusion(f32[2,128,1024]{2,1,0:T(8,128)S(1)} %copy-done.1, f32[2,128,1024]{2,1,0:T(8,128)S(1)} %copy-done.2, s32[128]{0:T(128)S(1)} %iota_add_fusion), kind=kOutput, calls=%fused_computation.58 | convolution fusion | flops 1610874880 | bytes 5243392 | tf_op jit(solution)/shard_map/dot_general | solution.py:14
  214.9 5.4 %copy.4 = f32[1024,1024]{0,1:T(8,128)} copy(f32[1024,1024]{1,0:T(8,128)} %fusion.60) | data formatting | bytes 8388608 | tf_op jit(solution)/shard_map/dot_general | solution.py:14
  220.3 14.8 %collective-permute-done.3 = f32[128,1024]{1,0:T(8,128)} collective-permute-done((f32[128,1024]{1,0:T(8,128)S(1)}, f32[128,1024]{1,0:T(8,128)}, u32[]{:S(2)}, u32[]{:S(2)}) %collective-permute-start.3) | collective-permute-done | bytes 524320 | tf_op jit(solution)/shard_map/ppermute | solution.py:28
  235.2 4.7 %fusion.53 = f32[1024,1024]{1,0:T(8,128)S(1)} fusion(f32[2,128,1024]{2,1,0:T(8,128)S(1)} %copy-done.1, f32[128,1024]{1,0:T(8,128)S(1)} %fusion.6, f32[128,1024]{1,0:T(8,128)} %collective-permute-done.3, f32[128,1024]{1,0:T(8,128)} %collective-permute-done.4, pred[]{:T(512)S(6)} %eq.31), kind=kOutput, calls=%fused_computation.51 | convolution fusion | flops 1610874880 | bytes 6291457 | tf_op jit(solution)/shard_map/dot_general | solution.py:14
  241.8 16.6 %fusion.14 = f32[1024,1024]{1,0:T(8,128)} fusion(f32[1024,1024]{1,0:T(8,128)S(1)} %fusion.53, f32[2,1024,1024]{2,1,0:T(8,128)} %all-gather.2.cloned.1.call-done), kind=kOutput, calls=%fused_computation.15 | convolution fusion | flops 12886999040 | bytes 12582912 | tf_op jit(solution)/shard_map/dot_general | solution.py:14
  258.4 5.4 %copy.6 = f32[1024,1024]{0,1:T(8,128)} copy(f32[1024,1024]{1,0:T(8,128)} %fusion.14) | data formatting | bytes 8388608 | tf_op jit(solution)/shard_map/dot_general | solution.py:14
  263.8 10.7 %fusion.3 = f32[1024,1024]{1,0:T(8,128)} fusion(f32[1024,1024]{1,0:T(8,128)} %copy-done, f32[1024,1024]{1,0:T(8,128)} %fusion.60, f32[1024,1024]{0,1:T(8,128)} %copy.6, f32[1024,1024]{1,0:T(8,128)} %fusion.14, f32[1024,1024]{0,1:T(8,128)} %copy.4, pred[]{:T(512)S(6)} %eq.31), kind=kLoop, calls=%fused_computation.4 | loop fusion | flops 16777216 | bytes 25165824 | tf_op jit(solution)/shard_map/jit(_where)/select_n | solution.py:71
  274.5 48.7 %reduce-scatter.9.cloned.1.call-done = f32[128,1024]{1,0:T(8,128)} async-done(((f32[1024,1024]{1,0:T(8,128)}), f32[128,1024]{1,0:T(8,128)}) %reduce-scatter.9.cloned.1.call-update) | async-done | bytes 524304 | tf_op jit(solution)/shard_map/reduce_scatter | solution.py:71
  323.2 4.8 %fusion.4 = f32[128,1024]{1,0:T(8,128)S(1)} fusion(f32[128,1024]{1,0:T(8,128)} %reduce-scatter.9.cloned.1.call-done, f32[2,1024,1024]{2,1,0:T(8,128)} %param.5), kind=kOutput, calls=%fused_computation.5 | convolution fusion | flops 1610612736 | bytes 5242880 | tf_op jit(solution)/shard_map/dot_general | solution.py:10
  328.0 6.3 %fusion.51 = f32[1024,1024]{1,0:T(8,128)} fusion(f32[128,1024]{1,0:T(8,128)S(1)} %fusion.4, f32[1,1024,1024]{2,1,0:T(8,128)} %get-tuple-element.13, s32[]{:T(128)S(6)} %select_n.91), kind=kOutput, calls=%fused_computation.49 | convolution fusion | flops 1610612736 | bytes 5242884 | tf_op jit(solution)/shard_map/dot_general | solution.py:14
  334.3 51.5 %reduce-scatter.11.cloned.1.call-done = f32[128,1024]{1,0:T(8,128)} async-done(((f32[1024,1024]{1,0:T(8,128)}), f32[128,1024]{1,0:T(8,128)}) %reduce-scatter.11.cloned.1.call-update) | async-done | bytes 524304 | tf_op jit(solution)/shard_map/reduce_scatter | solution.py:74
  388.6 5.3 %fusion.43 = f32[1,128,1024]{2,1,0:T(8,128)S(1)} fusion(f32[128,1024]{1,0:T(8,128)S(1)} %fusion.46, f32[2,1024,1024]{2,1,0:T(8,128)} %all-gather.2.cloned.1.call-done, f32[128,1024]{1,0:T(8,128)S(1)} %copy-done.4, s32[128]{0:T(128)S(1)} %iota_add_fusion, pred[]{:T(512)S(6)} %eq.31, pred[]{:T(512)S(6)} %lt.8, f32[128,1024]{1,0:T(8,128)S(1)} %fusion.6, ...), kind=kOutput, calls=%fused_computation.42 | convolution fusion | flops 1612185600 | bytes 8914944 | tf_op jit(solution)/shard_map/dot_general | solution.py:10
  393.9 19.9 %collective-permute-done.5 = f32[128,1024]{1,0:T(8,128)} collective-permute-done((f32[128,1024]{1,0:T(8,128)}, f32[128,1024]{1,0:T(8,128)}, u32[]{:S(2)}, u32[]{:S(2)}) %collective-permute-start.5) | collective-permute-done | bytes 524320 | tf_op jit(solution)/shard_map/ppermute | solution.py:28
  413.8 5.0 %fusion.34 = f32[1,128,1024]{2,1,0:T(8,128)S(1)} fusion(f32[2,1024,1024]{2,1,0:T(8,128)} %all-gather.2.cloned.1.call-done, f32[128,1024]{1,0:T(8,128)S(1)} %copy-done.3, f32[128,1024]{1,0:T(8,128)S(1)} %copy-done.5, f32[128,1024]{1,0:T(8,128)} %collective-permute-done.5, f32[128,1024]{1,0:T(8,128)} %collective-permute-done.6, ...), kind=kOutput, calls=%fused_computation.39 | convolution fusion | flops 1612054528 | bytes 7866368 | tf_op jit(solution)/shard_map/dot_general | solution.py:10
  (38 shorter events, 21.0 us)
Async XLA Ops:
  6.5 72.5 %reduce-scatter.5.cloned.1.call-start = ((), (), s32[]{:S(2)}) async-start(), calls=%async_computation.4 | async-start | bytes 4718592 | tf_op jit(solution)/shard_map/reduce_scatter | solution.py:56
  24.8 116.6 %reduce-scatter.7.cloned.1.call-start = ((), (), s32[]{:S(2)}) async-start(), calls=%async_computation.5 | async-start | bytes 4718592 | tf_op jit(solution)/shard_map/reduce_scatter | solution.py:58
  89.9 107.8 %copy-start.2 = (f32[2,128,1024]{2,1,0:T(8,128)S(1)}, f32[2,128,1024]{2,1,0:T(8,128)}, u32[]{:S(2)}) copy-start(f32[2,128,1024]{2,1,0:T(8,128)} %param.4) | copy-start | bytes 3145732
  89.9 107.8 %all-gather.2.cloned.1.call-start = ((), (), s32[]{:S(2)}) async-start(), calls=%async_computation.6 | async-start | bytes 9437184 | tf_op jit(solution)/shard_map/all_gather | solution.py:62
  141.4 181.7 %reduce-scatter.9.cloned.1.call-start = ((), (), s32[]{:S(2)}) async-start(), calls=%async_computation.7 | async-start | bytes 4718592 | tf_op jit(solution)/shard_map/reduce_scatter | solution.py:71
  141.5 2.9 collective-permute-start.2
  142.2 2.2 collective-permute-start.1
  142.9 38.7 %collective-permute-start = (f32[128,1024]{1,0:T(8,128)}, f32[128,1024]{1,0:T(8,128)S(1)}, u32[]{:S(2)}, u32[]{:S(2)}) collective-permute-start(f32[128,1024]{1,0:T(8,128)} %reduce-scatter.7.cloned.1.call-done), channel_id=1, source_target_pairs={{24,0},{25,1},{26,2},{27,3},{28,4},{29,5},{30,6},{31,7}} | collective-permute-start | bytes 1572872 | tf_op jit(solution)/shard_map/ppermute | solution.py:28
  181.7 28.0 %copy-start.1 = (f32[2,128,1024]{2,1,0:T(8,128)S(1)}, f32[2,128,1024]{2,1,0:T(8,128)}, u32[]{:S(2)}) copy-start(f32[2,128,1024]{2,1,0:T(8,128)} %param.3) | copy-start | bytes 3145732
  206.9 13.4 %collective-permute-start.4 = (f32[128,1024]{1,0:T(8,128)S(1)}, f32[128,1024]{1,0:T(8,128)}, u32[]{:S(2)}, u32[]{:S(2)}) collective-permute-start(f32[128,1024]{1,0:T(8,128)S(1)} %fusion.6), channel_id=1, source_target_pairs={{16,8},{17,9},{18,10},{19,11},{20,12},{21,13},{22,14},{23,15}} | collective-permute-start | bytes 1572872 | tf_op jit(solution)/shard_map/ppermute | solution.py:28
  208.4 26.8 %collective-permute-start.3 = (f32[128,1024]{1,0:T(8,128)S(1)}, f32[128,1024]{1,0:T(8,128)}, u32[]{:S(2)}, u32[]{:S(2)}) collective-permute-start(f32[128,1024]{1,0:T(8,128)S(1)} %fusion.6), channel_id=1, source_target_pairs={{16,0},{17,1},{18,2},{19,3},{20,4},{21,5},{22,6},{23,7}} | collective-permute-start | bytes 1572872 | tf_op jit(solution)/shard_map/ppermute | solution.py:28
  239.9 1.9 copy-start
  274.5 111.3 %reduce-scatter.11.cloned.1.call-start = ((), (), s32[]{:S(2)}) async-start(), calls=%async_computation.8 | async-start | bytes 4718592 | tf_op jit(solution)/shard_map/reduce_scatter | solution.py:74
  328.0 60.6 %copy-start.4 = (f32[128,1024]{1,0:T(8,128)S(1)}, f32[128,1024]{1,0:T(8,128)}, u32[]{:S(2)}) copy-start(f32[128,1024]{1,0:T(8,128)} %reduce-scatter.7.cloned.1.call-done) | copy-start | bytes 1572868
  334.3 79.5 %copy-start.3 = (f32[128,1024]{1,0:T(8,128)S(1)}, f32[128,1024]{1,0:T(8,128)}, u32[]{:S(2)}) copy-start(f32[128,1024]{1,0:T(8,128)} %reduce-scatter.9.cloned.1.call-done) | copy-start | bytes 1572868
  385.8 8.0 %collective-permute-start.6 = (f32[128,1024]{1,0:T(8,128)}, f32[128,1024]{1,0:T(8,128)}, u32[]{:S(2)}, u32[]{:S(2)}) collective-permute-start(f32[128,1024]{1,0:T(8,128)} %reduce-scatter.11.cloned.1.call-done), channel_id=1, source_target_pairs={{16,8},{17,9},{18,10},{19,11},{20,12},{21,13},{22,14},{23,15}} | collective-permute-start | bytes 1572872 | tf_op jit(solution)/shard_map/ppermute | solution.py:28
  387.3 26.5 %collective-permute-start.5 = (f32[128,1024]{1,0:T(8,128)}, f32[128,1024]{1,0:T(8,128)}, u32[]{:S(2)}, u32[]{:S(2)}) collective-permute-start(f32[128,1024]{1,0:T(8,128)} %reduce-scatter.11.cloned.1.call-done), channel_id=1, source_target_pairs={{16,0},{17,1},{18,2},{19,3},{20,4},{21,5},{22,6},{23,7}} | collective-permute-start | bytes 1572872 | tf_op jit(solution)/shard_map/ppermute | solution.py:28
  388.6 25.2 %copy-start.5 = (f32[128,1024]{1,0:T(8,128)S(1)}, f32[128,1024]{1,0:T(8,128)}, u32[]{:S(2)}) copy-start(f32[128,1024]{1,0:T(8,128)} %reduce-scatter.11.cloned.1.call-done) | copy-start | bytes 1572868
Sparse Core Ops, SparseCore 0:
  25.0 53.9 reduce-scatter.4
  90.1 51.3 reduce-scatter.6
  143.3 54.3 all-gather.1
  274.6 48.5 reduce-scatter.8
  334.4 51.3 reduce-scatter.10
